TPU v7x, 512 devices: a whole 4x8x8 slice. The times are simulated.
512 devices in a mesh: grp: 32 (over x, y), tp: 16 (over z, core).
Axes of the slice: x: 4, y: 8, z: 8, core: 2. Of those that a mesh axis runs over, the one named last changes fastest.
Arguments:
- patches: bfloat16 [16384, 1664], P('grp'), may hold values from -6 to 6
- patch_image: int32 [16384], P('grp'), may hold values from 0 to 4095, as said below
- vis_gain: float32 [1664], replicated, may hold values from 0.25 to 1.75
- vis_bias: float32 [1664], replicated, may hold values from -3 to 3
- vis_qkv: bfloat16 [3, 1664, 1664], P(None, None, 'tp'), may hold values from -2 to 2
- vis_out: bfloat16 [1664, 1664], P('tp'), may hold values from -0.15625 to 0.15625
- merge_weight: bfloat16 [4, 1664, 1024], P(None, 'tp'), may hold values from -0.078125 to 0.078125
- positions: int32 [4096], P('grp'), may hold values from 0 to 12287, as said below
- text: bfloat16 [8192, 1024], P('grp'), may hold values from -6 to 6
- dec_gain: float32 [1024], replicated, may hold values from 0.25 to 1.75
- dec_bias: float32 [1024], replicated, may hold values from -3 to 3
- dec_qkv: bfloat16 [3, 1024, 1024], P(None, None, 'tp'), may hold values from -2 to 2
Outputs:
- dec_attn: bfloat16 [12288, 1024], P('grp', 'tp')
Inputs may be any that keep to these rules, and one draw needn't show every extreme that they name: `patch_image`: each aligned run of four patches belongs to one image. Groups 2j and 2j+1 are partners: the last image of group 2j continues as the first image of group 2j+1; no other image is shared between groups. All positions are distinct; each group's block of 384 positions holds exactly 128 of them; the 128 merged rows of one group put at most 8 positions into any one group's block.
All inputs are finite; a program needn't handle non-finite values.
Results may differ from a plain program's by a relative error of at most 0.025.
Values may be sent and summed in bfloat16 or wider, within the bound.
No kernel may reach another device: no remote copies, remote signals or barrier semaphores. Data moves between devices by JAX's collectives and lax.ppermute only.
A program may use at most 128 MiB of HBM per device.

v0:
```python
import jax
import jax.numpy as jnp
from jax import lax
from jax.sharding import PartitionSpec as P

HD = 104
DH = 64
layer_eps = 1e-05


def swapped(value, axis, stride):
    return lax.ppermute(value, axis, [(i, i ^ 1 << stride) for i in range(lax.axis_size(axis))])


def normalize(values, gain, bias):
    mean = jnp.mean(values, axis=-1, keepdims=True)
    centred = values - mean
    spread = jnp.mean(centred * centred, axis=-1, keepdims=True)
    return centred * lax.rsqrt(spread + layer_eps) * gain + bias


def body(
    patches,
    patch_image,
    vis_gain,
    vis_bias,
    vis_qkv,
    vis_out,
    merge_weight,
    positions,
    text,
    dec_gain,
    dec_bias,
    dec_qkv,
):
    rows = patches.shape[0]
    heads = vis_qkv.shape[2] // HD
    patches_f = patches.astype(jnp.float32)
    normed = normalize(patches_f, vis_gain, vis_bias).astype(jnp.bfloat16)
    proj = jnp.einsum("pd,sde->spe", normed, vis_qkv, preferred_element_type=jnp.float32).astype(
        jnp.bfloat16
    )
    query = proj[0].reshape(rows, heads, HD)
    partner_kv, partner_ids = swapped((proj[1:], patch_image), "grp", 0)
    both_kv = jnp.concatenate([proj[1:], partner_kv], axis=1)
    both_ids = jnp.concatenate([patch_image, partner_ids], axis=0)
    keys = both_kv[0].reshape(2 * rows, heads, HD)
    values = both_kv[1].reshape(2 * rows, heads, HD)
    scores = jnp.einsum("phe,khe->hpk", query, keys, preferred_element_type=jnp.float32) * HD ** (
        -0.5
    )
    same = patch_image[:, None] == both_ids[None, :]
    top = jnp.max(jnp.where(same, scores, -1e30), axis=2, keepdims=True)
    expo = jnp.where(same, jnp.exp(scores - top), 0.0)
    weights = (expo / jnp.sum(expo, axis=2, keepdims=True)).astype(jnp.bfloat16)
    attended = jnp.einsum(
        "hpk,khe->phe", weights, values, preferred_element_type=jnp.float32
    ).astype(jnp.bfloat16)
    attended = attended.reshape(rows, heads * HD)
    width = patches.shape[1] // lax.axis_size("tp")
    mixed = lax.psum_scatter(
        lax.dot_general(
            vis_out, attended, (((0,), (1,)), ((), ())), preferred_element_type=jnp.float32
        ).astype(jnp.bfloat16),
        "tp",
        scatter_dimension=0,
        tiled=True,
    ).astype(jnp.float32)
    own_cols = lax.dynamic_slice_in_dim(patches_f, lax.axis_index("tp") * width, width, 1)
    visual = (mixed + own_cols.T).astype(jnp.bfloat16)
    windows = visual.reshape(width, rows // 4, 4)
    partial_rows = jnp.einsum(
        "cmk,kce->me", windows, merge_weight, preferred_element_type=jnp.float32
    )
    groups = lax.axis_size("grp")
    here = lax.axis_index("grp")
    merged_count = rows // 4
    text_count = text.shape[0]
    tok = text_count + merged_count
    cap = merged_count // min(groups, 16)
    target = positions // tok
    member = (target[:, None] == jnp.arange(groups, dtype=jnp.int32)[None, :]).astype(jnp.int32)
    rank = jnp.sum(jnp.cumsum(member, axis=0) * member, axis=1) - 1
    slot = target * cap + rank
    select = slot[None, :] == jnp.arange(groups * cap, dtype=jnp.int32)[:, None]
    select_bf = select.astype(jnp.bfloat16)
    bucket_pos = jnp.sum(jnp.where(select, positions[None, :] + 1, 0), axis=1) - 1
    merged = lax.psum(partial_rows.astype(jnp.bfloat16), "tp")
    packed = jnp.dot(select_bf, merged, preferred_element_type=jnp.float32).astype(jnp.bfloat16)
    got_rows, got_pos = (
        lax.all_to_all(packed, "grp", split_axis=0, concat_axis=0, tiled=True),
        lax.all_to_all(bucket_pos, "grp", split_axis=0, concat_axis=0, tiled=True),
    )
    local_pos = got_pos - here * tok
    place = jnp.arange(tok, dtype=jnp.int32)
    landing = (local_pos[None, :] == place[:, None]) & (got_pos[None, :] >= 0)
    image_here = jnp.any(landing, axis=1).astype(jnp.int32)
    text_index = place - (jnp.cumsum(image_here) - image_here)
    text_pick = (image_here[:, None] == 0) & (
        text_index[:, None] == jnp.arange(text_count, dtype=jnp.int32)[None, :]
    )
    prompt = jnp.dot(landing.astype(jnp.bfloat16), got_rows, preferred_element_type=jnp.float32)
    prompt = prompt + jnp.dot(
        text_pick.astype(jnp.bfloat16), text, preferred_element_type=jnp.float32
    )
    dnorm = normalize(prompt, dec_gain, dec_bias).astype(jnp.bfloat16)
    dproj = jnp.einsum("td,sde->ste", dnorm, dec_qkv, preferred_element_type=jnp.float32).astype(
        jnp.bfloat16
    )
    dheads = dec_qkv.shape[2] // DH
    dquery = dproj[0].reshape(tok, dheads, DH)
    query_pos = here * tok + place
    best = jnp.full((dheads, tok), -1e30, jnp.float32)
    key_rows = lax.all_gather(dproj[1], "grp", axis=0, tiled=True).reshape(-1, dheads, DH)
    value_rows = lax.all_gather(dproj[2], "grp", axis=0, tiled=True).reshape(-1, dheads, DH)
    key_pos = jnp.arange(key_rows.shape[0], dtype=jnp.int32)
    score = jnp.einsum(
        "the,rhe->htr", dquery, key_rows, preferred_element_type=jnp.float32
    ) * DH ** (-0.5)
    allowed = key_pos[None, :] <= query_pos[:, None]
    new_best = jnp.maximum(best, jnp.max(jnp.where(allowed[None], score, -1e30), axis=2))
    expo_d = jnp.where(allowed[None], jnp.exp(score - new_best[:, :, None]), 0.0)
    total = jnp.sum(expo_d, axis=2)
    acc = jnp.einsum(
        "htr,rhe->hte", expo_d.astype(jnp.bfloat16), value_rows, preferred_element_type=jnp.float32
    )
    best, total, acc = (new_best, total, acc)
    result = acc / total[:, :, None]
    return result.transpose(1, 0, 2).reshape(tok, dheads * DH).astype(jnp.bfloat16)


def solution(mesh):
    in_specs = (
        P("grp", None),
        P("grp"),
        P(),
        P(),
        P(None, None, "tp"),
        P("tp", None),
        P(None, "tp", None),
        P("grp"),
        P("grp", None),
        P(),
        P(),
        P(None, None, "tp"),
    )
    out_specs = P("grp", "tp")
    return jax.shard_map(body, mesh=mesh, in_specs=in_specs, out_specs=out_specs, check_vma=False)
```

profile of v0, /device:TPU:8, one launch (start us, length us, event | category | flops | bytes accessed | tf_op | source)
XLA Modules:
  0.0 415.6 jit_solution(2915710087922539153)
XLA Ops:
  6.6 1.9 convert_reduce_fusion
  8.6 0.6 multiply_reduce_fusion
  9.2 1.0 fusion.6
  10.3 7.7 %collective-permute-start = (bf16[2,512,104]{1,2,0:T(8,128)(2,1)S(1)}, bf16[2,512,104]{1,2,0:T(8,128)(2,1)S(1)}, u32[]{:S(2)}, u32[]{:S(2)}) collective-permute-start(bf16[2,512,104]{1,2,0:T(8,128)(2,1)S(1)} %slice.38), channel_id=1, source_target_pairs={{0,16},{16,0},{32,48},{48,32},{64,80},{80,64},{96,112},{112,96},{1... | collective-permute-start | bytes 638984 | tf_op jit(solution)/shard_map/ppermute | solution.py:12
  18.1 1.9 collective-permute-start.1
  20.0 3.6 collective-permute-done.1
  23.6 0.6 fusion.5
  24.2 1.4 copy-done.2
  25.5 0.7 fusion.13
  26.2 4.3 %fusion.4 = bf16[1664,512]{0,1:T(8,128)(2,1)} fusion(bf16[104,1664]{1,0:T(8,128)(2,1)S(1)} %copy-done.6, f32[512,1024]{1,0:T(8,128)} %copy-done.2, f32[512]{0:T(512)S(1)} %fusion.13, f32[512]{0:T(512)S(1)} %get-tuple-element.11, s32[1024]{0:T(1024)S(1)} %pad_add_fusion, s32[512]{0:T(512)S(1)} %copy-done.4, bf16[2,512,104]{1,2,0:T(8,128)(2,1)S(1)} %slice.38, ...), kind=kOutput, calls=%fused_computation.10 | convolution fusion | flops 290738176 | bytes 4583424 | tf_op jit(solution)/shard_map/dot_general | solution.py:62
  30.5 3.6 copy.17
  34.2 2.0 convert_element_type.82
  36.8 59.7 %reduce-scatter.4.cloned.1.call-done = bf16[104,512]{1,0:T(8,128)(2,1)} async-done(((bf16[1664,512]{1,0:T(8,128)(2,1)}), bf16[104,512]{1,0:T(8,128)(2,1)}) %reduce-scatter.4.cloned.1.call-update) | async-done | bytes 106512
  96.5 1.0 copy.18
  97.5 1.2 fusion.49
  98.7 2.2 fusion.15
  100.9 0.7 sub.80
  101.6 9.9 %all-to-all-start = ((s32[32,8,1]{1,2,0:T(1,128)}), s32[32,8,1]{1,2,0:T(1,128)S(1)}, u32[]{:S(2)}, u32[]{:S(2)}) async-start(s32[32,8,1]{1,2,0:T(1,128)} %bitcast), calls=%async_computation | async-start | bytes 32768 | tf_op jit(solution)/shard_map/all_to_all | solution.py:92
  111.5 102.0 %all-reduce.2.cloned.1.call-done = bf16[128,1024]{1,0:T(8,128)(2,1)} async-done(((bf16[128,1024]{1,0:T(8,128)(2,1)}), bf16[128,1024]{1,0:T(8,128)(2,1)}) %all-reduce.2.cloned.1.call-update) | async-done | bytes 262160 | tf_op jit(solution)/shard_map/psum | solution.py:88
  213.5 2.0 fusion.14
  215.5 9.8 %all-to-all-start.1 = ((bf16[32,8,1024]{2,1,0:T(8,128)(2,1)}), bf16[32,8,1024]{2,1,0:T(8,128)(2,1)S(1)}, u32[]{:S(2)}, u32[]{:S(2)}) async-start(bf16[32,8,1024]{2,1,0:T(8,128)(2,1)} %fusion.14), calls=%async_computation.1 | async-start | bytes 1048576 | tf_op jit(solution)/shard_map/all_to_all | solution.py:91
  226.5 16.5 %all-to-all-done.1 = bf16[32,8,1024]{2,1,0:T(8,128)(2,1)S(1)} async-done(((bf16[32,8,1024]{2,1,0:T(8,128)(2,1)}), bf16[32,8,1024]{2,1,0:T(8,128)(2,1)S(1)}, u32[]{:S(2)}, u32[]{:S(2)}) %all-to-all-start.1) | async-done | bytes 524320 | tf_op jit(solution)/shard_map/all_to_all | solution.py:91
  243.0 0.4 fusion.42
  243.4 0.5 fusion.75
  244.4 0.5 fusion.37
  245.0 0.6 fusion.74
  245.9 0.3 all-gather.7.cloned.1.call-update
  246.3 71.2 %all-gather.5.cloned.1.call-done = bf16[1,12288,64]{1,2,0:T(8,128)(2,1)} async-done(((bf16[1,384,64]{1,2,0:T(8,128)(2,1)}), bf16[1,12288,64]{1,2,0:T(8,128)(2,1)}) %all-gather.5.cloned.1.call-update) | async-done | bytes 1572880 | tf_op jit(solution)/shard_map/all_gather | solution.py:114
  317.4 9.3 %select_reduce_fusion = (f32[384]{0:T(512)S(1)}, f32[384,12288]{1,0:T(8,128)}) fusion(s32[384]{0:T(512)S(1)} %iota_add_fusion, bf16[1,12288,64]{1,2,0:T(8,128)(2,1)} %all-gather.5.cloned.1.call-done, bf16[3,384,64]{1,2,0:T(8,128)(2,1)S(1)} %convert_bitcast_fusion.1), kind=kOutput, calls=%fused_computation.1 | convolution fusion | flops 622853760 | bytes 20499968 | tf_op jit(solution)/shard_map/the,rhe->htr/dot_general | solution.py:117
  326.7 11.1 %fusion = f32[384]{0:T(512)S(1)} fusion(f32[384,12288]{1,0:T(8,128)} %get-tuple-element.16, f32[384]{0:T(512)S(1)} %broadcast_maximum_fusion, s32[384]{0:T(512)S(1)} %iota_add_fusion), kind=kLoop, calls=%fused_computation.4 | loop fusion | flops 18873984 | bytes 18878976 | tf_op jit(solution)/shard_map/reduce_sum | solution.py:123
  337.8 60.2 %all-gather.7.cloned.1.call-done = bf16[1,12288,64]{1,2,0:T(8,128)(2,1)} async-done(((bf16[1,384,64]{1,2,0:T(8,128)(2,1)}), bf16[1,12288,64]{1,2,0:T(8,128)(2,1)}) %all-gather.7.cloned.1.call-update) | async-done | bytes 1572880 | tf_op jit(solution)/shard_map/all_gather | solution.py:115
  398.0 11.1 %fusion.22 = bf16[384,64]{0,1:T(8,128)(2,1)} fusion(bf16[1,12288,64]{1,2,0:T(8,128)(2,1)} %all-gather.7.cloned.1.call-done, f32[384,12288]{1,0:T(8,128)} %get-tuple-element.16, f32[384]{0:T(512)S(1)} %broadcast_maximum_fusion, s32[384]{0:T(512)S(1)} %iota_add_fusion, f32[384]{0:T(512)S(1)} %fusion), kind=kOutput, calls=%fused_computation.34 | convolution fusion | flops 622903296 | bytes 20500992 | tf_op jit(solution)/shard_map/htr,rhe->hte/dot_general | solution.py:124
  (61 shorter events, 2.8 us)
Async XLA Ops:
  6.5 2.6 copy-start
  6.5 2.1 copy-start.1
  6.5 2.7 copy-start.8
  6.5 2.7 copy-start.7
  6.5 89.9 %reduce-scatter.4.cloned.1.call-start = ((), (), s32[]{:S(2)}) async-start(), calls=%async_computation.6 | async-start | bytes 1810432
  9.2 8.9 %copy-start.4 = (s32[512]{0:T(512)S(1)}, s32[512]{0:T(512)}, u32[]{:S(2)}) copy-start(s32[512]{0:T(512)} %param.13) | copy-start | bytes 6148
  10.3 13.2 %collective-permute-start = (bf16[2,512,104]{1,2,0:T(8,128)(2,1)S(1)}, bf16[2,512,104]{1,2,0:T(8,128)(2,1)S(1)}, u32[]{:S(2)}, u32[]{:S(2)}) collective-permute-start(bf16[2,512,104]{1,2,0:T(8,128)(2,1)S(1)} %slice.38), channel_id=1, source_target_pairs={{0,16},{16,0},{32,48},{48,32},{64,80},{80,64},{96,112},{112,96},{1... | collective-permute-start | bytes 638984 | tf_op jit(solution)/shard_map/ppermute | solution.py:12
  18.1 5.5 %collective-permute-start.1 = (s32[512]{0:T(512)S(1)}, s32[512]{0:T(512)S(1)}, u32[]{:S(2)}, u32[]{:S(2)}) collective-permute-start(s32[512]{0:T(512)S(1)} %copy-done.4), channel_id=1, source_target_pairs={{0,16},{16,0},{32,48},{48,32},{64,80},{80,64},{96,112},{112,96},{1... | collective-permute-start | bytes 6152 | tf_op jit(solution)/shard_map/ppermute | solution.py:12
  23.6 2.6 copy-start.6
  24.2 1.4 copy-start.2
  34.1 179.3 %all-reduce.2.cloned.1.call-start = ((), (), s32[]{:S(2)}) async-start(), calls=%async_computation.3 | async-start | bytes 524288 | tf_op jit(solution)/shard_map/psum | solution.py:88
  34.2 2.0 copy-start.11
  100.9 142.5 %copy-start.3 = (bf16[256,1024]{1,0:T(8,128)(2,1)S(1)}, bf16[256,1024]{1,0:T(8,128)(2,1)}, u32[]{:S(2)}) copy-start(bf16[256,1024]{1,0:T(8,128)(2,1)} %param.20) | copy-start | bytes 1572868
  101.6 113.9 %all-to-all-start = ((s32[32,8,1]{1,2,0:T(1,128)}), s32[32,8,1]{1,2,0:T(1,128)S(1)}, u32[]{:S(2)}, u32[]{:S(2)}) async-start(s32[32,8,1]{1,2,0:T(1,128)} %bitcast), calls=%async_computation | async-start | bytes 32768 | tf_op jit(solution)/shard_map/all_to_all | solution.py:92
  215.5 27.5 %all-to-all-start.1 = ((bf16[32,8,1024]{2,1,0:T(8,128)(2,1)}), bf16[32,8,1024]{2,1,0:T(8,128)(2,1)S(1)}, u32[]{:S(2)}, u32[]{:S(2)}) async-start(bf16[32,8,1024]{2,1,0:T(8,128)(2,1)} %fusion.14), calls=%async_computation.1 | async-start | bytes 1048576 | tf_op jit(solution)/shard_map/all_to_all | solution.py:91
  225.4 92.1 %all-gather.5.cloned.1.call-start = ((), (), s32[]{:S(2)}) async-start(), calls=%async_computation.4 | async-start | bytes 1622016 | tf_op jit(solution)/shard_map/all_gather | solution.py:114
  243.4 1.0 copy-start.5
  243.4 1.0 copy-start.9
  243.4 1.0 copy-start.10
  245.7 152.3 %all-gather.7.cloned.1.call-start = ((), (), s32[]{:S(2)}) async-start(), calls=%async_computation.5 | async-start | bytes 1622016 | tf_op jit(solution)/shard_map/all_gather | solution.py:115
Sparse Core Ops, SparseCore 0:
  34.3 62.1 reduce-scatter.3
  101.0 112.4 all-reduce.1
  245.8 71.5 all-gather.4
  320.4 77.5 all-gather.6
where the time goes:
time: 416 us
  waiting for transfers between devices  313 us (75%)
  matrix products  32 us (8%)
  starting transfers between devices  29.7 us (7%)
  other arithmetic  19 us (5%)
  between operations  13.4 us (3%)
  local copies, waits for them, and re-layouts  8.01 us (2%)
    psum x1, waiting for transfers between devices, body(): merged = lax.psum(partial_rows.astype(jnp.bfloat16), 'tp')  102 us
    all_gather x1, waiting for transfers between devices, body(): lax.all_gather(dproj[1], 'grp', axis=0, tiled=True).reshape(-1, dheads, DH)  71.2 us
    all_gather x1, waiting for transfers between devices, body(): lax.all_gather(dproj[2], 'grp', axis=0, tiled=True).reshape(-1, dheads, DH)  60.2 us
    unnamed x5, waiting for transfers between devices  60.1 us
    all_to_all x1, waiting for transfers between devices, body(): lax.all_to_all(packed, 'grp', split_axis=0, concat_axis=0, tiled=True)  16.5 us
    dot_general x1, matrix products, body(): jnp.einsum('htr,rhe->hte', expo_d.astype(jnp.bfloat16), value_rows, prefe...  11.1 us
    reduce_sum x1, other arithmetic, body(): total = jnp.sum(expo_d, axis=2)  11.1 us
    all_to_all x1, starting transfers between devices, body(): lax.all_to_all(bucket_pos, 'grp', split_axis=0, concat_axis=0, tiled=True)  9.88 us
  transfers between devices with their start and end apart: 8, of which 6 were waited for; matrix products, arithmetic and copies ran while one was open for 6% of the time, Pallas kernels for 0%

commit v1 on v0

--- a/solution.py
+++ b/solution.py
@@ -85,7 +85,7 @@
     select = slot[None, :] == jnp.arange(groups * cap, dtype=jnp.int32)[:, None]
     select_bf = select.astype(jnp.bfloat16)
     bucket_pos = jnp.sum(jnp.where(select, positions[None, :] + 1, 0), axis=1) - 1
-    merged = lax.psum(partial_rows.astype(jnp.bfloat16), "tp")
+    merged = jnp.sum(lax.all_gather(partial_rows.astype(jnp.bfloat16), "tp"), axis=0)
     packed = jnp.dot(select_bf, merged, preferred_element_type=jnp.float32).astype(jnp.bfloat16)
     got_rows, got_pos = (
         lax.all_to_all(packed, "grp", split_axis=0, concat_axis=0, tiled=True),

time: 416 us -> 350 us (0.84)
  waiting for transfers between devices: 313 us -> 245 us
    psum x1 -> x0, waiting for transfers between devices: 102 us -> none  [body(): merged = lax.psum(partial_rows.astype(jnp.bfloat16), 'tp')]
    all_gather x0 -> x1, waiting for transfers between devices: none -> 32.5 us  [body(): lax.all_gather(partial_rows.astype(jnp.bfloat16), 'tp')]
  transfers between devices with their start and end apart: 8 -> 8, of which waited for: 6 -> 6; matrix products, arithmetic and copies ran while one was open for 6% -> 8% of each run, Pallas kernels for 0% -> 0%
where the time goes in v1:
time: 350 us; the launch traced here: 349 us
  waiting for transfers between devices  245 us (70%)
  matrix products  31 us (9%)
  starting transfers between devices  29.7 us (8%)
  other arithmetic  22.2 us (6%)
  between operations  13.4 us (4%)
  local copies, waits for them, and re-layouts  8.01 us (2%)
    all_gather x1, waiting for transfers between devices, body(): lax.all_gather(dproj[1], 'grp', axis=0, tiled=True).reshape(-1, dheads, DH)  70.8 us
    unnamed x5, waiting for transfers between devices  60.7 us
    all_gather x1, waiting for transfers between devices, body(): lax.all_gather(dproj[2], 'grp', axis=0, tiled=True).reshape(-1, dheads, DH)  60.6 us
    all_gather x1, waiting for transfers between devices, body(): lax.all_gather(partial_rows.astype(jnp.bfloat16), 'tp')  32.5 us
    all_to_all x1, waiting for transfers between devices, body(): lax.all_to_all(packed, 'grp', split_axis=0, concat_axis=0, tiled=True)  16.9 us
    dot_general x1, matrix products, body(): jnp.einsum('htr,rhe->hte', expo_d.astype(jnp.bfloat16), value_rows, prefe...  11.1 us
    reduce_sum x1, other arithmetic, body(): total = jnp.sum(expo_d, axis=2)  11.1 us
    all_to_all x1, starting transfers between devices, body(): lax.all_to_all(bucket_pos, 'grp', split_axis=0, concat_axis=0, tiled=True)  9.88 us
  transfers between devices with their start and end apart: 8, of which 6 were waited for; matrix products, arithmetic and copies ran while one was open for 8% of the time, Pallas kernels for 0%

profile of v1, /device:TPU:8, one launch (start us, length us, event | category | flops | bytes accessed | tf_op | source)
XLA Modules:
  0.0 349.4 jit_solution(18053819068211594260)
XLA Ops:
  6.6 1.9 convert_reduce_fusion
  8.6 0.6 multiply_reduce_fusion
  9.2 1.0 fusion.6
  10.3 7.7 %collective-permute-start = (bf16[2,512,104]{1,2,0:T(8,128)(2,1)S(1)}, bf16[2,512,104]{1,2,0:T(8,128)(2,1)S(1)}, u32[]{:S(2)}, u32[]{:S(2)}) collective-permute-start(bf16[2,512,104]{1,2,0:T(8,128)(2,1)S(1)} %slice.38), channel_id=1, source_target_pairs={{0,16},{16,0},{32,48},{48,32},{64,80},{80,64},{96,112},{112,96},{1... | collective-permute-start | bytes 638984 | tf_op jit(solution)/shard_map/ppermute | solution.py:12
  18.1 1.9 collective-permute-start.1
  20.0 3.6 %collective-permute-done.1 = s32[512]{0:T(512)S(1)} collective-permute-done((s32[512]{0:T(512)S(1)}, s32[512]{0:T(512)S(1)}, u32[]{:S(2)}, u32[]{:S(2)}) %collective-permute-start.1) | collective-permute-done | bytes 2080 | tf_op jit(solution)/shard_map/ppermute | solution.py:12
  23.6 0.6 fusion.5
  24.2 1.4 copy-done.2
  25.5 0.7 fusion.13
  26.2 4.3 %fusion.4 = bf16[1664,512]{0,1:T(8,128)(2,1)} fusion(bf16[104,1664]{1,0:T(8,128)(2,1)S(1)} %copy-done.6, f32[512,1024]{1,0:T(8,128)} %copy-done.2, f32[512]{0:T(512)S(1)} %fusion.13, f32[512]{0:T(512)S(1)} %get-tuple-element.11, s32[1024]{0:T(1024)S(1)} %pad_add_fusion, s32[512]{0:T(512)S(1)} %copy-done.4, bf16[2,512,104]{1,2,0:T(8,128)(2,1)S(1)} %slice.38, ...), kind=kOutput, calls=%fused_computation.10 | convolution fusion | flops 290738176 | bytes 4583424 | tf_op jit(solution)/shard_map/dot_general | solution.py:62
  30.5 3.6 %copy.19 = bf16[1664,512]{1,0:T(8,128)(2,1)} copy(bf16[1664,512]{0,1:T(8,128)(2,1)} %fusion.4) | data formatting | bytes 3407872
  34.2 2.0 convert_element_type.84
  36.2 60.3 %reduce-scatter.4.cloned.1.call-done = bf16[104,512]{1,0:T(8,128)(2,1)} async-done(((bf16[1664,512]{1,0:T(8,128)(2,1)}), bf16[104,512]{1,0:T(8,128)(2,1)}) %reduce-scatter.4.cloned.1.call-update) | async-done | bytes 106512
  96.5 1.0 copy.20
  97.5 1.2 fusion.49
  98.7 2.2 fusion.15
  101.5 0.7 sub.80
  102.2 9.9 %all-to-all-start = ((s32[32,8,1]{1,2,0:T(1,128)}), s32[32,8,1]{1,2,0:T(1,128)S(1)}, u32[]{:S(2)}, u32[]{:S(2)}) async-start(s32[32,8,1]{1,2,0:T(1,128)} %bitcast), calls=%async_computation | async-start | bytes 32768 | tf_op jit(solution)/shard_map/all_to_all | solution.py:92
  112.1 32.5 %all-gather.7.cloned.1.call-done = bf16[2048,1024]{1,0:T(8,128)(2,1)} async-done(((bf16[128,1024]{1,0:T(8,128)(2,1)}), bf16[2048,1024]{1,0:T(8,128)(2,1)}) %all-gather.7.cloned.1.call-update) | async-done | bytes 4194320 | tf_op jit(solution)/shard_map/all_gather | solution.py:88
  144.6 3.1 reduce_sum.89
  147.7 1.1 fusion.14
  148.8 9.8 %all-to-all-start.1 = ((bf16[32,8,1024]{2,1,0:T(8,128)(2,1)}), bf16[32,8,1024]{2,1,0:T(8,128)(2,1)S(1)}, u32[]{:S(2)}, u32[]{:S(2)}) async-start(bf16[32,8,1024]{2,1,0:T(8,128)(2,1)} %fusion.14), calls=%async_computation.1 | async-start | bytes 1048576 | tf_op jit(solution)/shard_map/all_to_all | solution.py:91
  159.8 16.9 %all-to-all-done.1 = bf16[32,8,1024]{2,1,0:T(8,128)(2,1)S(1)} async-done(((bf16[32,8,1024]{2,1,0:T(8,128)(2,1)}), bf16[32,8,1024]{2,1,0:T(8,128)(2,1)S(1)}, u32[]{:S(2)}, u32[]{:S(2)}) %all-to-all-start.1) | async-done | bytes 524320 | tf_op jit(solution)/shard_map/all_to_all | solution.py:91
  176.7 0.4 fusion.42
  177.2 0.5 fusion.75
  178.1 0.5 fusion.37
  178.7 0.6 fusion.74
  180.0 70.8 %all-gather.9.cloned.1.call-done = bf16[1,12288,64]{1,2,0:T(8,128)(2,1)} async-done(((bf16[1,384,64]{1,2,0:T(8,128)(2,1)}), bf16[1,12288,64]{1,2,0:T(8,128)(2,1)}) %all-gather.9.cloned.1.call-update) | async-done | bytes 1572880 | tf_op jit(solution)/shard_map/all_gather | solution.py:114
  250.7 9.3 %select_reduce_fusion = (f32[384]{0:T(512)S(1)}, f32[384,12288]{1,0:T(8,128)}) fusion(s32[384]{0:T(512)S(1)} %iota_add_fusion, bf16[1,12288,64]{1,2,0:T(8,128)(2,1)} %all-gather.9.cloned.1.call-done, bf16[3,384,64]{1,2,0:T(8,128)(2,1)S(1)} %convert_bitcast_fusion.1), kind=kOutput, calls=%fused_computation.1 | convolution fusion | flops 622853760 | bytes 20499968 | tf_op jit(solution)/shard_map/the,rhe->htr/dot_general | solution.py:117
  260.0 11.1 %fusion = f32[384]{0:T(512)S(1)} fusion(f32[384,12288]{1,0:T(8,128)} %get-tuple-element.16, f32[384]{0:T(512)S(1)} %broadcast_maximum_fusion, s32[384]{0:T(512)S(1)} %iota_add_fusion), kind=kLoop, calls=%fused_computation.4 | loop fusion | flops 18873984 | bytes 18878976 | tf_op jit(solution)/shard_map/reduce_sum | solution.py:123
  271.1 60.6 %all-gather.11.cloned.1.call-done = bf16[1,12288,64]{1,2,0:T(8,128)(2,1)} async-done(((bf16[1,384,64]{1,2,0:T(8,128)(2,1)}), bf16[1,12288,64]{1,2,0:T(8,128)(2,1)}) %all-gather.11.cloned.1.call-update) | async-done | bytes 1572880 | tf_op jit(solution)/shard_map/all_gather | solution.py:115
  331.8 11.1 %fusion.22 = bf16[384,64]{0,1:T(8,128)(2,1)} fusion(bf16[1,12288,64]{1,2,0:T(8,128)(2,1)} %all-gather.11.cloned.1.call-done, f32[384,12288]{1,0:T(8,128)} %get-tuple-element.16, f32[384]{0:T(512)S(1)} %broadcast_maximum_fusion, s32[384]{0:T(512)S(1)} %iota_add_fusion, f32[384]{0:T(512)S(1)} %fusion), kind=kOutput, calls=%fused_computation.34 | convolution fusion | flops 622903296 | bytes 20500992 | tf_op jit(solution)/shard_map/htr,rhe->hte/dot_general | solution.py:124
  (62 shorter events, 3.1 us)
Async XLA Ops:
  6.5 2.6 copy-start
  6.5 2.1 copy-start.1
  6.5 2.7 copy-start.8
  6.5 2.7 copy-start.7
  6.5 89.9 %reduce-scatter.4.cloned.1.call-start = ((), (), s32[]{:S(2)}) async-start(), calls=%async_computation.6 | async-start | bytes 1810432
  9.2 8.9 %copy-start.4 = (s32[512]{0:T(512)S(1)}, s32[512]{0:T(512)}, u32[]{:S(2)}) copy-start(s32[512]{0:T(512)} %param.13) | copy-start | bytes 6148
  10.3 13.2 %collective-permute-start = (bf16[2,512,104]{1,2,0:T(8,128)(2,1)S(1)}, bf16[2,512,104]{1,2,0:T(8,128)(2,1)S(1)}, u32[]{:S(2)}, u32[]{:S(2)}) collective-permute-start(bf16[2,512,104]{1,2,0:T(8,128)(2,1)S(1)} %slice.38), channel_id=1, source_target_pairs={{0,16},{16,0},{32,48},{48,32},{64,80},{80,64},{96,112},{112,96},{1... | collective-permute-start | bytes 638984 | tf_op jit(solution)/shard_map/ppermute | solution.py:12
  18.1 5.5 %collective-permute-start.1 = (s32[512]{0:T(512)S(1)}, s32[512]{0:T(512)S(1)}, u32[]{:S(2)}, u32[]{:S(2)}) collective-permute-start(s32[512]{0:T(512)S(1)} %copy-done.4), channel_id=1, source_target_pairs={{0,16},{16,0},{32,48},{48,32},{64,80},{80,64},{96,112},{112,96},{1... | collective-permute-start | bytes 6152 | tf_op jit(solution)/shard_map/ppermute | solution.py:12
  23.6 2.6 copy-start.6
  24.2 1.4 copy-start.2
  34.1 110.5 %all-gather.7.cloned.1.call-start = ((), (), s32[]{:S(2)}) async-start(), calls=%async_computation.3 | async-start | bytes 4456448 | tf_op jit(solution)/shard_map/all_gather | solution.py:88
  36.2 64.7 %copy-start.11 = (s32[128]{0:T(128)S(1)}, s32[128]{0:T(128)}, u32[]{:S(2)}) copy-start(s32[128]{0:T(128)} %param.19) | copy-start | bytes 1540
  102.2 46.6 %all-to-all-start = ((s32[32,8,1]{1,2,0:T(1,128)}), s32[32,8,1]{1,2,0:T(1,128)S(1)}, u32[]{:S(2)}, u32[]{:S(2)}) async-start(s32[32,8,1]{1,2,0:T(1,128)} %bitcast), calls=%async_computation | async-start | bytes 32768 | tf_op jit(solution)/shard_map/all_to_all | solution.py:92
  147.7 29.4 %copy-start.3 = (bf16[256,1024]{1,0:T(8,128)(2,1)S(1)}, bf16[256,1024]{1,0:T(8,128)(2,1)}, u32[]{:S(2)}) copy-start(bf16[256,1024]{1,0:T(8,128)(2,1)} %param.20) | copy-start | bytes 1572868
  148.8 27.9 %all-to-all-start.1 = ((bf16[32,8,1024]{2,1,0:T(8,128)(2,1)}), bf16[32,8,1024]{2,1,0:T(8,128)(2,1)S(1)}, u32[]{:S(2)}, u32[]{:S(2)}) async-start(bf16[32,8,1024]{2,1,0:T(8,128)(2,1)} %fusion.14), calls=%async_computation.1 | async-start | bytes 1048576 | tf_op jit(solution)/shard_map/all_to_all | solution.py:91
  158.7 92.1 %all-gather.9.cloned.1.call-start = ((), (), s32[]{:S(2)}) async-start(), calls=%async_computation.4 | async-start | bytes 1622016 | tf_op jit(solution)/shard_map/all_gather | solution.py:114
  177.1 1.0 copy-start.5
  177.1 1.0 copy-start.9
  177.2 1.0 copy-start.10
  179.4 152.4 %all-gather.11.cloned.1.call-start = ((), (), s32[]{:S(2)}) async-start(), calls=%async_computation.5 | async-start | bytes 1622016 | tf_op jit(solution)/shard_map/all_gather | solution.py:115
Sparse Core Ops, SparseCore 0:
  34.3 62.1 reduce-scatter.3
  101.0 43.5 all-gather.6
  179.5 71.1 all-gather.8
  254.2 77.5 all-gather.10
